TPU v7x, 128 devices: a whole 4x4x4 slice. The times are simulated.
128 devices in a mesh: row: 8 (over z, core), col: 16 (over x, y).
Axes of the slice: x: 4, y: 4, z: 4, core: 2. Of those that a mesh axis runs over, the one named last changes fastest.
Arguments:
- snapshots: float32 [512, 196608], P(('row', 'col')), may hold values from -6 to 6
- panels: float32 [8, 6, 32768, 256], P(None, None, ('row', 'col')), may hold values from -0.1875 to 0.1875
- diag_inverse: float32 [8, 256, 256], replicated, may hold values from -0.6 to 1.5, as said below
Outputs:
- whitened: float32 [6, 32768, 512], P(None, ('row', 'col'))
Inputs may be any that keep to these rules, and one draw needn't show every extreme that they name: Each block of diag_inverse is lower triangular with a diagonal of 0.5 to 1.5.
All inputs are finite; a program needn't handle non-finite values.
Results may differ from a plain program's by a relative error of at most 0.0001.
Values sent between devices are 32-bit elements; how exact they have to be, the bound alone decides.
No kernel may reach another device: no remote copies, remote signals or barrier semaphores. Data moves between devices by JAX's collectives and lax.ppermute only.
A program may use at most 128 MiB of HBM per device.

v0:
```python
import jax
import jax.numpy as jnp
from jax import lax
from jax.sharding import PartitionSpec as P


def spread(block, axis, owner):
    block = jnp.where(lax.axis_index(axis) == owner, block, jnp.zeros_like(block))
    return lax.psum(block, axis)


def per_device(snapshots, panels, diag_inverse):
    local_count, order_size = snapshots.shape
    sections, blocks, width_block, _ = panels.shape
    devices = lax.axis_size(("row", "col"))
    pieces = snapshots.reshape(local_count, blocks, devices, width_block)
    arrived = lax.all_to_all(pieces, ("row", "col"), split_axis=2, concat_axis=0, tiled=True)
    remaining = jnp.transpose(
        arrived.reshape(devices * local_count, blocks, width_block), (1, 2, 0)
    )
    device = lax.axis_index(("row", "col"))
    block_owner = lax.broadcasted_iota(jnp.int32, (blocks, 1, 1), 0) * devices + device
    for section in range(sections):
        solved = jnp.dot(
            diag_inverse[section],
            remaining[0],
            precision=lax.Precision.HIGHEST,
            preferred_element_type=jnp.float32,
        )
        solved = spread(solved, ("row", "col"), section)
        product = jnp.einsum(
            "jrc,cs->jrs",
            panels[section],
            solved,
            precision=lax.Precision.HIGHEST,
            preferred_element_type=jnp.float32,
        )
        remaining = jnp.where(
            block_owner > section,
            remaining - product,
            jnp.where(block_owner == section, solved[None], remaining),
        )
    return remaining


def solution(mesh):
    in_specs = (P(("row", "col"), None), P(None, None, ("row", "col"), None), P())
    out_specs = P(None, ("row", "col"), None)
    return jax.shard_map(
        per_device, mesh=mesh, in_specs=in_specs, out_specs=out_specs, check_vma=False
    )
```

profile of v0, /device:TPU:1, one launch (start us, length us, event | category | flops | bytes accessed | tf_op | source)
XLA Modules:
  0.0 1303.0 jit_solution(7980638426046954538)
XLA Ops:
  6.5 2.5 copy.19
  9.0 3.7 copy.12
  12.7 11.5 all-to-all-start
  24.2 0.0 all-reduce.9.cloned.1.call-start
  24.3 41.0 %all-to-all-done = f32[4,6,128,256]{3,0,1,2:T(4,128)S(1)} async-done(((f32[4,6,128,256]{3,0,1,2:T(4,128)}), f32[4,6,128,256]{3,0,1,2:T(4,128)S(1)}, u32[]{:S(2)}, u32[]{:S(2)}) %all-to-all-start) | async-done | bytes 3145760 | tf_op jit(solution)/shard_map/all_to_all | solution.py:17
  65.3 2.2 copy.13
  67.5 3.2 reshape.70
  70.7 2.6 convolution_select_fusion.7
  73.3 0.5 all-reduce.11.cloned.1.call-start
  73.8 141.1 %all-reduce.9.cloned.1.call-done = f32[256,512]{1,0:T(8,128)} async-done(((f32[256,512]{1,0:T(8,128)}), f32[256,512]{1,0:T(8,128)}) %all-reduce.9.cloned.1.call-update) | async-done | bytes 524304 | tf_op jit(solution)/shard_map/psum | solution.py:9
  214.9 2.0 copy.15
  216.9 8.6 fusion.7
  225.6 2.4 fusion.30
  227.9 0.0 all-reduce.11.cloned.1.call-update
  227.9 0.0 all-reduce.13.cloned.1.call-start
  228.0 143.9 %all-reduce.11.cloned.1.call-done = f32[256,512]{0,1:T(8,128)} async-done(((f32[256,512]{0,1:T(8,128)}), f32[256,512]{0,1:T(8,128)}) %all-reduce.11.cloned.1.call-update) | async-done | bytes 524304 | tf_op jit(solution)/shard_map/psum | solution.py:9
  371.9 4.8 fusion.6
  376.7 1.7 copy-done
  378.4 2.4 fusion.29
  380.7 0.0 all-reduce.13.cloned.1.call-update
  380.8 0.2 all-reduce.15.cloned.1.call-start
  381.0 143.7 %all-reduce.13.cloned.1.call-done = f32[256,512]{0,1:T(8,128)} async-done(((f32[256,512]{0,1:T(8,128)}), f32[256,512]{0,1:T(8,128)}) %all-reduce.13.cloned.1.call-update) | async-done | bytes 524304 | tf_op jit(solution)/shard_map/psum | solution.py:9
  524.7 5.5 fusion.5
  530.3 2.4 fusion.28
  532.7 0.0 all-reduce.15.cloned.1.call-update
  532.7 0.0 all-reduce.17.cloned.1.call-start
  532.8 143.9 %all-reduce.15.cloned.1.call-done = f32[256,512]{0,1:T(8,128)} async-done(((f32[256,512]{0,1:T(8,128)}), f32[256,512]{0,1:T(8,128)}) %all-reduce.15.cloned.1.call-update) | async-done | bytes 524304 | tf_op jit(solution)/shard_map/psum | solution.py:9
  676.7 4.8 fusion.4
  681.5 1.7 copy-done.1
  683.1 2.4 fusion.27
  685.5 0.0 all-reduce.19.cloned.1.call-start
  685.6 143.9 %all-reduce.17.cloned.1.call-done = f32[256,512]{0,1:T(8,128)} async-done(((f32[256,512]{0,1:T(8,128)}), f32[256,512]{0,1:T(8,128)}) %all-reduce.17.cloned.1.call-update) | async-done | bytes 524304 | tf_op jit(solution)/shard_map/psum | solution.py:9
  829.5 5.5 fusion.3
  835.0 2.4 fusion.26
  837.4 0.0 all-reduce.19.cloned.1.call-update
  837.4 0.3 all-reduce.21.cloned.1.call-start
  837.7 143.8 %all-reduce.19.cloned.1.call-done = f32[256,512]{0,1:T(8,128)} async-done(((f32[256,512]{0,1:T(8,128)}), f32[256,512]{0,1:T(8,128)}) %all-reduce.19.cloned.1.call-update) | async-done | bytes 524304 | tf_op jit(solution)/shard_map/psum | solution.py:9
  981.5 4.8 fusion.2
  986.3 1.7 copy-done.2
  987.9 2.4 fusion.25
  990.3 0.0 all-reduce.23.cloned.1.call-start
  990.4 143.9 %all-reduce.21.cloned.1.call-done = f32[256,512]{0,1:T(8,128)} async-done(((f32[256,512]{0,1:T(8,128)}), f32[256,512]{0,1:T(8,128)}) %all-reduce.21.cloned.1.call-update) | async-done | bytes 524304 | tf_op jit(solution)/shard_map/psum | solution.py:9
  1134.3 5.5 fusion.1
  1139.8 2.4 fusion.24
  1142.2 0.0 all-reduce.23.cloned.1.call-update
  1142.2 143.9 %all-reduce.23.cloned.1.call-done = f32[256,512]{0,1:T(8,128)} async-done(((f32[256,512]{0,1:T(8,128)}), f32[256,512]{0,1:T(8,128)}) %all-reduce.23.cloned.1.call-update) | async-done | bytes 524304 | tf_op jit(solution)/shard_map/psum | solution.py:9
  1286.2 6.3 fusion
  1292.4 3.5 copy.16
  (16 shorter events, 0.1 us)
Async XLA Ops:
  12.7 52.5 %all-to-all-start = ((f32[4,6,128,256]{3,0,1,2:T(4,128)}), f32[4,6,128,256]{3,0,1,2:T(4,128)S(1)}, u32[]{:S(2)}, u32[]{:S(2)}) async-start(f32[4,6,128,256]{3,0,1,2:T(4,128)} %copy.12), calls=%async_computation | async-start | bytes 6291456 | tf_op jit(solution)/shard_map/all_to_all | solution.py:17
  24.2 190.7 %all-reduce.9.cloned.1.call-start = ((), (), s32[]{:S(2)}) async-start(), calls=%async_computation.1 | async-start | bytes 1048576 | tf_op jit(solution)/shard_map/psum | solution.py:9
  70.7 146.3 %copy-start.3 = (f32[512,6,256]{2,0,1:T(8,128)}, f32[512,6,256]{2,0,1:T(8,128)S(1)}, u32[]{:S(2)}) copy-start(f32[512,6,256]{2,0,1:T(8,128)S(1)} %reshape.70) | copy-start | bytes 9437188
  73.3 298.6 %all-reduce.11.cloned.1.call-start = ((), (), s32[]{:S(2)}) async-start(), calls=%async_computation.2 | async-start | bytes 1048576 | tf_op jit(solution)/shard_map/psum | solution.py:9
  227.9 296.8 %all-reduce.13.cloned.1.call-start = ((), (), s32[]{:S(2)}) async-start(), calls=%async_computation.3 | async-start | bytes 1048576 | tf_op jit(solution)/shard_map/psum | solution.py:9
  376.7 1.7 copy-start
  380.8 295.9 %all-reduce.15.cloned.1.call-start = ((), (), s32[]{:S(2)}) async-start(), calls=%async_computation.4 | async-start | bytes 1048576 | tf_op jit(solution)/shard_map/psum | solution.py:9
  532.7 296.8 %all-reduce.17.cloned.1.call-start = ((), (), s32[]{:S(2)}) async-start(), calls=%async_computation.5 | async-start | bytes 1048576 | tf_op jit(solution)/shard_map/psum | solution.py:9
  681.4 1.7 copy-start.1
  685.5 296.0 %all-reduce.19.cloned.1.call-start = ((), (), s32[]{:S(2)}) async-start(), calls=%async_computation.6 | async-start | bytes 1048576 | tf_op jit(solution)/shard_map/psum | solution.py:9
  837.4 296.8 %all-reduce.21.cloned.1.call-start = ((), (), s32[]{:S(2)}) async-start(), calls=%async_computation.7 | async-start | bytes 1048576 | tf_op jit(solution)/shard_map/psum | solution.py:9
  986.2 1.7 copy-start.2
  990.3 295.9 %all-reduce.23.cloned.1.call-start = ((), (), s32[]{:S(2)}) async-start(), calls=%async_computation.8 | async-start | bytes 1048576 | tf_op jit(solution)/shard_map/psum | solution.py:9
Sparse Core Ops, SparseCore 0:
  73.4 141.4 all-reduce.8
  228.1 143.8 all-reduce.10
  380.9 143.8 all-reduce.12
  532.8 143.8 all-reduce.14
  685.6 143.8 all-reduce.16
  837.6 143.8 all-reduce.18
  990.4 143.7 all-reduce.20
  1142.3 143.7 all-reduce.22
where the time goes:
time: 1310 us; the launch traced here: 1300 us
  waiting for transfers between devices  1190 us (91%)
  matrix products  65 us (5%)
  local copies, waits for them, and re-layouts  22.1 us (2%)
  between operations  13.9 us (1%)
    psum x8, waiting for transfers between devices, spread(): return lax.psum(block, axis)  1150 us
    dot_general x8, matrix products, per_device(): jnp.einsum('jrc,cs->jrs', panels[section], solved, precision=lax.Precisio...  45.8 us
    all_to_all x1, waiting for transfers between devices, per_device(): lax.all_to_all(pieces, ('row', 'col'), split_axis=2, concat_axis=0, tiled...  41 us
  transfers between devices with their start and end apart: 9, of which 9 were waited for; matrix products, arithmetic and copies ran while one was open for 0% of the time, Pallas kernels for 0%

commit v1 on v0

--- a/solution.py
+++ b/solution.py
@@ -2,6 +2,18 @@
 import jax.numpy as jnp
 from jax import lax
 from jax.sharding import PartitionSpec as P
+
+
+def view_the_patch(piece_in):
+    return jnp.concatenate(
+        lax.all_to_all(
+            jnp.stack(jnp.split(piece_in, lax.axis_size(("row", "col")), axis=2), axis=0),
+            ("row", "col"),
+            0,
+            0,
+        ),
+        axis=0,
+    )
 
 
 def spread(block, axis, owner):
@@ -14,7 +26,7 @@
     sections, blocks, width_block, _ = panels.shape
     devices = lax.axis_size(("row", "col"))
     pieces = snapshots.reshape(local_count, blocks, devices, width_block)
-    arrived = lax.all_to_all(pieces, ("row", "col"), split_axis=2, concat_axis=0, tiled=True)
+    arrived = view_the_patch(pieces)
     remaining = jnp.transpose(
         arrived.reshape(devices * local_count, blocks, width_block), (1, 2, 0)
     )

time: 1310 us -> 1310 us (level)
  no operation moved by 1% of the time
where the time goes in v1:
time: 1310 us; the launch traced here: 1300 us
  waiting for transfers between devices  1190 us (91%)
  matrix products  62 us (5%)
  local copies, waits for them, and re-layouts  22.9 us (2%)
  between operations  14.3 us (1%)
    psum x8, waiting for transfers between devices, spread(): return lax.psum(block, axis)  1150 us
    dot_general x8, matrix products, per_device(): jnp.einsum('jrc,cs->jrs', panels[section], solved, precision=lax.Precisio...  42.8 us
    all_to_all x1, waiting for transfers between devices, view_the_patch(): lax.all_to_all(jnp.stack(jnp.split(piece_in, lax.axis_size(('row', 'col')...  41 us
  transfers between devices with their start and end apart: 9, of which 9 were waited for; matrix products, arithmetic and copies ran while one was open for 0% of the time, Pallas kernels for 0%

profile of v1, /device:TPU:1, one launch (start us, length us, event | category | flops | bytes accessed | tf_op | source)
XLA Modules:
  0.0 1301.2 jit_solution(635419692808135040)
XLA Ops:
  6.5 2.5 copy.138
  13.5 2.5 copy.135
  15.9 11.5 all-to-all-start
  27.4 0.0 all-reduce.9.cloned.1.call-start
  27.5 41.0 %all-to-all-done = f32[128,4,6,1,256]{4,1,2,3,0:T(4,128)S(1)} async-done(((f32[128,4,6,1,256]{4,1,2,3,0:T(4,128)}), f32[128,4,6,1,256]{4,1,2,3,0:T(4,128)S(1)}, u32[]{:S(2)}, u32[]{:S(2)}) %all-to-all-start) | async-done | bytes 3145760 | tf_op jit(solution)/shard_map/all_to_all | solution.py:9
  68.5 2.2 copy.136
  70.7 3.2 reshape_reshape.3
  73.9 2.6 fusion.31
  76.5 0.0 all-reduce.9.cloned.1.call-update
  76.5 0.0 all-reduce.11.cloned.1.call-start
  76.5 141.5 %all-reduce.9.cloned.1.call-done = f32[256,512]{0,1:T(8,128)} async-done(((f32[256,512]{0,1:T(8,128)}), f32[256,512]{0,1:T(8,128)}) %all-reduce.9.cloned.1.call-update) | async-done | bytes 524304 | tf_op jit(solution)/shard_map/psum | solution.py:21
  218.1 5.6 fusion.7
  223.7 2.4 fusion.30
  226.1 0.0 all-reduce.11.cloned.1.call-update
  226.1 0.5 all-reduce.13.cloned.1.call-start
  226.7 143.4 %all-reduce.11.cloned.1.call-done = f32[256,512]{0,1:T(8,128)} async-done(((f32[256,512]{0,1:T(8,128)}), f32[256,512]{0,1:T(8,128)}) %all-reduce.11.cloned.1.call-update) | async-done | bytes 524304 | tf_op jit(solution)/shard_map/psum | solution.py:21
  370.1 4.8 fusion.6
  374.9 1.7 copy-done
  376.5 2.4 fusion.29
  378.9 0.0 all-reduce.13.cloned.1.call-update
  378.9 0.0 all-reduce.15.cloned.1.call-start
  379.0 143.9 %all-reduce.13.cloned.1.call-done = f32[256,512]{0,1:T(8,128)} async-done(((f32[256,512]{0,1:T(8,128)}), f32[256,512]{0,1:T(8,128)}) %all-reduce.13.cloned.1.call-update) | async-done | bytes 524304 | tf_op jit(solution)/shard_map/psum | solution.py:21
  522.9 5.5 fusion.5
  528.5 2.4 fusion.28
  530.8 0.0 all-reduce.15.cloned.1.call-update
  530.8 0.0 all-reduce.17.cloned.1.call-start
  530.9 143.9 %all-reduce.15.cloned.1.call-done = f32[256,512]{0,1:T(8,128)} async-done(((f32[256,512]{0,1:T(8,128)}), f32[256,512]{0,1:T(8,128)}) %all-reduce.15.cloned.1.call-update) | async-done | bytes 524304 | tf_op jit(solution)/shard_map/psum | solution.py:21
  674.8 4.8 fusion.4
  679.6 1.7 copy-done.1
  681.2 2.4 fusion.27
  683.6 0.0 all-reduce.17.cloned.1.call-update
  683.6 0.2 all-reduce.19.cloned.1.call-start
  683.9 143.7 %all-reduce.17.cloned.1.call-done = f32[256,512]{0,1:T(8,128)} async-done(((f32[256,512]{0,1:T(8,128)}), f32[256,512]{0,1:T(8,128)}) %all-reduce.17.cloned.1.call-update) | async-done | bytes 524304 | tf_op jit(solution)/shard_map/psum | solution.py:21
  827.6 5.5 fusion.3
  833.2 2.4 fusion.26
  835.5 0.0 all-reduce.19.cloned.1.call-update
  835.6 0.0 all-reduce.21.cloned.1.call-start
  835.6 143.9 %all-reduce.19.cloned.1.call-done = f32[256,512]{0,1:T(8,128)} async-done(((f32[256,512]{0,1:T(8,128)}), f32[256,512]{0,1:T(8,128)}) %all-reduce.19.cloned.1.call-update) | async-done | bytes 524304 | tf_op jit(solution)/shard_map/psum | solution.py:21
  979.5 4.8 fusion.2
  984.3 1.7 copy-done.2
  986.0 2.4 fusion.25
  988.4 0.3 all-reduce.23.cloned.1.call-start
  988.7 143.7 %all-reduce.21.cloned.1.call-done = f32[256,512]{0,1:T(8,128)} async-done(((f32[256,512]{0,1:T(8,128)}), f32[256,512]{0,1:T(8,128)}) %all-reduce.21.cloned.1.call-update) | async-done | bytes 524304 | tf_op jit(solution)/shard_map/psum | solution.py:21
  1132.4 5.5 fusion.1
  1137.9 2.4 fusion.24
  1140.3 144.0 %all-reduce.23.cloned.1.call-done = f32[256,512]{0,1:T(8,128)} async-done(((f32[256,512]{0,1:T(8,128)}), f32[256,512]{0,1:T(8,128)}) %all-reduce.23.cloned.1.call-update) | async-done | bytes 524304 | tf_op jit(solution)/shard_map/psum | solution.py:21
  1284.3 6.2 fusion
  1290.6 3.5 copy.137
  (143 shorter events, 4.2 us)
Async XLA Ops:
  15.9 52.5 %all-to-all-start = ((f32[128,4,6,1,256]{4,1,2,3,0:T(4,128)}), f32[128,4,6,1,256]{4,1,2,3,0:T(4,128)S(1)}, u32[]{:S(2)}, u32[]{:S(2)}) async-start(f32[128,4,6,1,256]{4,1,2,3,0:T(4,128)} %copy.135), calls=%async_computation | async-start | bytes 6291456 | tf_op jit(solution)/shard_map/all_to_all | solution.py:9
  27.4 190.6 %all-reduce.9.cloned.1.call-start = ((), (), s32[]{:S(2)}) async-start(), calls=%async_computation.1 | async-start | bytes 1048576 | tf_op jit(solution)/shard_map/psum | solution.py:21
  73.9 144.2 %copy-start.3 = (f32[512,6,256]{2,0,1:T(8,128)}, f32[512,6,256]{2,0,1:T(8,128)S(1)}, u32[]{:S(2)}) copy-start(f32[512,6,256]{2,0,1:T(8,128)S(1)} %reshape_reshape.3) | copy-start | bytes 9437188
  76.5 293.6 %all-reduce.11.cloned.1.call-start = ((), (), s32[]{:S(2)}) async-start(), calls=%async_computation.2 | async-start | bytes 1048576 | tf_op jit(solution)/shard_map/psum | solution.py:21
  226.1 296.8 %all-reduce.13.cloned.1.call-start = ((), (), s32[]{:S(2)}) async-start(), calls=%async_computation.3 | async-start | bytes 1048576 | tf_op jit(solution)/shard_map/psum | solution.py:21
  374.9 1.7 copy-start
  378.9 295.9 %all-reduce.15.cloned.1.call-start = ((), (), s32[]{:S(2)}) async-start(), calls=%async_computation.4 | async-start | bytes 1048576 | tf_op jit(solution)/shard_map/psum | solution.py:21
  530.8 296.8 %all-reduce.17.cloned.1.call-start = ((), (), s32[]{:S(2)}) async-start(), calls=%async_computation.5 | async-start | bytes 1048576 | tf_op jit(solution)/shard_map/psum | solution.py:21
  679.6 1.7 copy-start.1
  683.6 295.9 %all-reduce.19.cloned.1.call-start = ((), (), s32[]{:S(2)}) async-start(), calls=%async_computation.6 | async-start | bytes 1048576 | tf_op jit(solution)/shard_map/psum | solution.py:21
  835.6 296.8 %all-reduce.21.cloned.1.call-start = ((), (), s32[]{:S(2)}) async-start(), calls=%async_computation.7 | async-start | bytes 1048576 | tf_op jit(solution)/shard_map/psum | solution.py:21
  984.3 1.7 copy-start.2
  988.4 296.0 %all-reduce.23.cloned.1.call-start = ((), (), s32[]{:S(2)}) async-start(), calls=%async_computation.8 | async-start | bytes 1048576 | tf_op jit(solution)/shard_map/psum | solution.py:21
Sparse Core Ops, SparseCore 0:
  76.6 141.4 all-reduce.8
  226.2 143.7 all-reduce.10
  379.0 143.8 all-reduce.12
  531.0 143.7 all-reduce.14
  683.8 143.8 all-reduce.16
  835.7 143.8 all-reduce.18
  988.5 143.8 all-reduce.20
  1140.4 143.8 all-reduce.22
